TPU v7x, 128 devices: a whole 4x4x4 slice. The times are simulated.
128 devices in a mesh: row: 4 (over z_lo, core), col: 4 (over x), slab: 8 (over y, z_hi).
Axes of the slice: x: 4, y: 4, z: 4 (z_hi: 2, z_lo: 2; z = z_hi * 2 + z_lo), core: 2. Of those that a mesh axis runs over, the one named last changes fastest.
Arguments:
- amplitudes: bfloat16 [48, 48, 480, 128], P('row', 'col', 'slab'), may hold values from -6 to 6
- integrals: bfloat16 [48, 480, 48, 128], P('row', 'slab', 'col'), may hold values from -0.0625 to 0.0625
- irreps: int32 [19], replicated, may hold values from 0 to 1
- pair_mask: int32 [4, 4], replicated, may hold values 0 or 1
Outputs:
- cycle_term: bfloat16 [48, 48, 128, 128], P('row', 'col', 'slab')
Inputs may be any that keep to these rules, and one draw needn't show every extreme that they name: Each label is one of the two irreps of the point group. `pair_mask`: 1 marks a block pair whose amplitudes are kept.
All inputs are finite; a program needn't handle non-finite values.
Results may differ from a plain program's by a relative error of at most 0.001.
Values may be sent and summed in bfloat16 or wider, within the bound.
No kernel may reach another device: no remote copies, remote signals or barrier semaphores. Data moves between devices by JAX's collectives and lax.ppermute only.
A program may use at most 128 MiB of HBM per device.

v0:
```python
import jax
import jax.numpy as jnp
from jax import lax
from jax.sharding import PartitionSpec as P

OBLK = 12
VTILE = 32


def swapped(value, axis, stride):
    mask = 2**stride
    pairs = [(source, source ^ mask) for source in range(lax.axis_size(axis))]
    return lax.ppermute(value, axis, pairs)


def block_onehot(first_row, row_count, blocks, block_width):
    block_ids = (first_row + jnp.arange(row_count, dtype=jnp.int32)) // block_width
    return (block_ids[:, None] == jnp.arange(blocks, dtype=jnp.int32)[None, :]).astype(jnp.float32)


def contract(amp_piece, int_piece, i_start, k_start, pair_mask):
    i_rows = amp_piece.shape[0]
    k_count = amp_piece.shape[1]
    blocks = pair_mask.shape[0]
    factor = jnp.dot(
        jnp.dot(block_onehot(i_start, i_rows, blocks, OBLK), pair_mask.astype(jnp.float32)),
        block_onehot(k_start, k_count, blocks, OBLK).T,
    )
    masked = amp_piece * factor.astype(jnp.bfloat16)[:, :, None, None]
    return jnp.einsum("ikca,kcjb->ijab", masked, int_piece, preferred_element_type=jnp.float32)


def body(amplitudes, integrals, irreps, pair_mask):
    i_rows, k_rows, c_cols, win_cols = amplitudes.shape
    j_rows = integrals.shape[2]
    blocks = pair_mask.shape[0]
    row_at = lax.axis_index("row")
    col_at = lax.axis_index("col")
    slab_at = lax.axis_index("slab")
    i_start = row_at * i_rows
    occ_labels = irreps[:blocks].astype(jnp.float32)
    vir_labels = irreps[blocks:].astype(jnp.float32)
    vir_tiles = vir_labels.shape[0]
    label_k = jnp.dot(
        block_onehot(row_at * integrals.shape[0], integrals.shape[0], blocks, OBLK), occ_labels
    )
    label_c = jnp.dot(block_onehot(slab_at * c_cols, c_cols, vir_tiles, VTILE), vir_labels)
    label_j = jnp.dot(block_onehot(col_at * j_rows, j_rows, blocks, OBLK), occ_labels)
    label_b = jnp.dot(block_onehot(0, win_cols, vir_tiles, VTILE), vir_labels)
    parity = (
        label_k[:, None, None, None]
        + label_c[None, :, None, None]
        + label_j[None, None, :, None]
        + label_b[None, None, None, :]
    )
    screened = jnp.where(jnp.remainder(parity, 2.0) == 0.0, integrals, jnp.zeros_like(integrals))
    int_whole = lax.all_gather(screened, "row", axis=0, tiled=True)
    cycle_part = contract(
        lax.all_gather(amplitudes, "col", axis=1, tiled=True),
        int_whole,
        i_start,
        jnp.int32(0),
        pair_mask,
    )
    shares = lax.psum_scatter(cycle_part, "slab", scatter_dimension=2, tiled=True)
    spread = lax.all_to_all(shares, "slab", split_axis=3, concat_axis=2, tiled=True)
    mirrored = jnp.transpose(spread, (1, 0, 3, 2))
    for bit_no in range(lax.axis_size("row").bit_length() - 1):
        across = swapped(swapped(mirrored, "row", bit_no), "col", bit_no)
        differ = row_at // 2**bit_no % 2 != col_at // 2**bit_no % 2
        mirrored = jnp.where(differ, across, mirrored)
    return (shares + mirrored).astype(jnp.bfloat16)


def solution(mesh):
    return jax.shard_map(
        body,
        mesh=mesh,
        in_specs=(P("row", "col", "slab", None), P("row", "slab", "col", None), P(), P()),
        out_specs=P("row", "col", "slab", None),
        check_vma=False,
    )
```

profile of v0, /device:TPU:0, one launch (start us, length us, event | category | flops | bytes accessed | tf_op | source)
XLA Modules:
  0.0 556.6 jit_solution(18274877579923600509)
XLA Ops:
  6.5 0.7 all-gather.5.cloned.1.call-update
  7.4 0.2 convolution_bitcast_fusion
  7.6 0.2 convolution_bitcast_fusion.1
  7.8 0.2 convolution_bitcast_fusion.2
  8.0 0.2 convolution_bitcast_fusion.3
  8.4 5.2 fusion.9
  13.7 0.6 copy-done.1
  14.3 0.4 convolution_convert_fusion
  14.6 88.8 %all-gather.5.cloned.1.call-done = bf16[12,48,60,128]{3,2,1,0:T(8,128)(2,1)} async-done(((bf16[12,12,60,128]{3,2,1,0:T(8,128)(2,1)}), bf16[12,48,60,128]{3,2,1,0:T(8,128)(2,1)}) %all-gather.5.cloned.1.call-update) | async-done | bytes 8847376 | tf_op jit(solution)/shard_map/all_gather | solution.py:59
  103.4 91.3 %all-gather.3.cloned.1.call-done = bf16[48,60,12,128]{3,1,0,2:T(8,128)(2,1)} async-done(((bf16[12,60,12,128]{3,1,0,2:T(8,128)(2,1)}), bf16[48,60,12,128]{3,1,0,2:T(8,128)(2,1)}) %all-gather.3.cloned.1.call-update) | async-done | bytes 8847376 | tf_op jit(solution)/shard_map/all_gather | solution.py:57
  194.7 21.9 %fusion.10 = f32[12,12,128,128]{2,3,0,1:T(8,128)} fusion(bf16[12,48,60,128]{3,2,1,0:T(8,128)(2,1)} %all-gather.5.cloned.1.call-done, bf16[12,48]{1,0:T(8,128)(2,1)S(1)} %convolution_convert_fusion, bf16[48,60,12,128]{3,1,0,2:T(8,128)(2,1)} %all-gather.3.cloned.1.call-done), kind=kOutput, calls=%fused_computation.13 | convolution fusion | flops 13607239680 | bytes 27133056 | tf_op jit(solution)/shard_map/ikca,kcjb->ijab/dot_general | solution.py:30
  216.6 12.7 %copy.18 = f32[12,12,128,128]{3,1,0,2:T(8,128)} copy(f32[12,12,128,128]{2,3,0,1:T(8,128)} %fusion.10) | data formatting | bytes 18874368 | tf_op jit(solution)/shard_map/ikca,kcjb->ijab/transpose | solution.py:30
  229.3 153.7 %reduce-scatter.2.cloned.1.call-done = f32[12,12,16,128]{3,1,0,2:T(8,128)} async-done(((f32[12,12,128,128]{3,1,0,2:T(8,128)}), f32[12,12,16,128]{3,1,0,2:T(8,128)}) %reduce-scatter.2.cloned.1.call-update) | async-done | bytes 1179664 | tf_op jit(solution)/shard_map/reduce_scatter | solution.py:65
  383.1 14.2 %copy.19 = f32[12,12,16,128]{2,0,1,3:T(8,128)} copy(f32[12,12,16,128]{3,1,0,2:T(8,128)} %reduce-scatter.2.cloned.1.call-done) | data formatting | bytes 2359296 | tf_op jit(solution)/shard_map/reduce_scatter | solution.py:65
  397.3 8.8 %reshape.121 = f32[8,1,36864]{2,1,0:T(1,128)S(1)} reshape(f32[128,12,12,16]{3,2,1,0:T(8,128)} %bitcast.47) | data formatting | bytes 2359296
  406.1 20.4 %all_to_all.18 = f32[8,1,36864]{2,1,0:T(1,128)S(1)} all-to-all(f32[8,1,36864]{2,1,0:T(1,128)S(1)} %reshape.121), channel_id=1, replica_groups=mesh['row'=4,'col'=4,'slab'=8] {'slab'}, dimensions={0} | all-to-all | bytes 2359296 | tf_op jit(solution)/shard_map/all_to_all | solution.py:66
  426.5 0.5 broadcast.211
  427.0 3.4 reduce
  430.5 10.0 %reshape.122 = f32[128,12,12,16]{3,2,1,0:T(8,128)} reshape(f32[8,36864]{1,0:T(8,128)S(1)} %reduce) | data formatting | bytes 2359296
  440.5 13.8 %copy.38 = f32[12,12,16,8,16]{2,3,4,1,0:T(8,128)} copy(f32[12,12,16,8,16]{2,0,1,4,3:T(8,128)} %bitcast.48) | data formatting | bytes 2359296 | tf_op jit(solution)/shard_map/all_to_all | solution.py:66
  454.3 6.2 %all_to_all.16 = f32[12,12,128,16]{2,3,1,0:T(8,128)S(1)} reshape(f32[12,12,8,16,16]{3,2,4,1,0:T(8,128)} %bitcast.49) | data formatting | bytes 2359296 | tf_op jit(solution)/shard_map/all_to_all | solution.py:66
  460.5 0.1 copy.21
  460.8 2.8 collective-permute-done
  463.6 1.5 collective-permute-start.1
  465.1 26.5 %collective-permute-done.1 = f32[12,12,16,128]{3,2,1,0:T(8,128)S(1)} collective-permute-done((f32[12,12,16,128]{3,2,1,0:T(8,128)S(1)}, f32[12,12,16,128]{3,2,1,0:T(8,128)S(1)}, u32[]{:S(2)}, u32[]{:S(2)}) %collective-permute-start.1) | collective-permute-done | bytes 1179680 | tf_op jit(solution)/shard_map/ppermute | solution.py:13
  491.6 0.2 copy_select_fusion.1
  491.9 1.3 collective-permute-start.2
  493.2 25.9 %collective-permute-done.2 = f32[12,12,16,128]{3,2,1,0:T(8,128)S(1)} collective-permute-done((f32[12,12,16,128]{3,2,1,0:T(8,128)S(1)}, f32[12,12,16,128]{3,2,1,0:T(8,128)S(1)}, u32[]{:S(2)}, u32[]{:S(2)}) %collective-permute-start.2) | collective-permute-done | bytes 1179680 | tf_op jit(solution)/shard_map/ppermute | solution.py:13
  519.1 3.0 collective-permute-start.3
  522.1 24.8 %collective-permute-done.3 = f32[12,12,16,128]{3,2,1,0:T(8,128)S(1)} collective-permute-done((f32[12,12,16,128]{3,2,1,0:T(8,128)S(1)}, f32[12,12,16,128]{3,2,1,0:T(8,128)S(1)}, u32[]{:S(2)}, u32[]{:S(2)}) %collective-permute-start.3) | collective-permute-done | bytes 1179680 | tf_op jit(solution)/shard_map/ppermute | solution.py:13
  546.9 2.2 fusion.15
  549.1 1.0 copy.26
  (19 shorter events, 0.6 us)
Async XLA Ops:
  6.5 0.9 copy-start.2
  6.5 1.8 copy-start
  6.5 96.9 %all-gather.5.cloned.1.call-start = ((), (), s32[]{:S(2)}) async-start(), calls=%async_computation.3 | async-start | bytes 11796480 | tf_op jit(solution)/shard_map/all_gather | solution.py:59
  7.3 187.4 %all-gather.3.cloned.1.call-start = ((), (), s32[]{:S(2)}) async-start(), calls=%async_computation.2 | async-start | bytes 11796480 | tf_op jit(solution)/shard_map/all_gather | solution.py:57
  13.6 0.7 copy-start.1
  13.6 369.5 %reduce-scatter.2.cloned.1.call-start = ((), (), s32[]{:S(2)}) async-start(), calls=%async_computation.4 | async-start | bytes 14155776 | tf_op jit(solution)/shard_map/reduce_scatter | solution.py:65
  460.7 2.9 collective-permute-start
  463.6 28.0 %collective-permute-start.1 = (f32[12,12,16,128]{3,2,1,0:T(8,128)S(1)}, f32[12,12,16,128]{3,2,1,0:T(8,128)S(1)}, u32[]{:S(2)}, u32[]{:S(2)}) collective-permute-start(f32[12,12,16,128]{3,2,1,0:T(8,128)S(1)} %collective-permute-done), channel_id=1, source_target_pairs={{0,8},{8,0},{16,24},{24,16},{1,9},{9,1},{17,25},{25,17},{2,10},{10... | collective-permute-start | bytes 3538952 | tf_op jit(solution)/shard_map/ppermute | solution.py:13
  491.9 27.2 %collective-permute-start.2 = (f32[12,12,16,128]{3,2,1,0:T(8,128)S(1)}, f32[12,12,16,128]{3,2,1,0:T(8,128)S(1)}, u32[]{:S(2)}, u32[]{:S(2)}) collective-permute-start(f32[12,12,16,128]{3,2,1,0:T(8,128)S(1)} %copy.23), channel_id=1, source_target_pairs={{0,64},{32,96},{64,0},{96,32},{1,65},{33,97},{65,1},{97,33},{2,66}... | collective-permute-start | bytes 3538952 | tf_op jit(solution)/shard_map/ppermute | solution.py:13
  519.1 27.8 %collective-permute-start.3 = (f32[12,12,16,128]{3,2,1,0:T(8,128)S(1)}, f32[12,12,16,128]{3,2,1,0:T(8,128)S(1)}, u32[]{:S(2)}, u32[]{:S(2)}) collective-permute-start(f32[12,12,16,128]{3,2,1,0:T(8,128)S(1)} %collective-permute-done.2), channel_id=1, source_target_pairs={{0,16},{8,24},{16,0},{24,8},{1,17},{9,25},{17,1},{25,9},{2,18},{10... | collective-permute-start | bytes 3538952 | tf_op jit(solution)/shard_map/ppermute | solution.py:13
Sparse Core Ops, SparseCore 0:
  9.0 94.3 all-gather.4
  105.1 89.5 all-gather.2
  229.4 153.5 reduce-scatter.1
where the time goes:
time: 557 us
  waiting for transfers between devices  415 us (75%)
  local copies, waits for them, and re-layouts  68.1 us (12%)
  matrix products  23.1 us (4%)
  blocking collectives  20.4 us (4%)
  between operations  13.2 us (2%)
  other arithmetic  11.2 us (2%)
  starting transfers between devices  6.01 us (1%)
    reduce_scatter x1, waiting for transfers between devices, body(): lax.psum_scatter(cycle_part, 'slab', scatter_dimension=2, tiled=True)  154 us
    all_gather x1, waiting for transfers between devices, body(): int_whole = lax.all_gather(screened, 'row', axis=0, tiled=True)  91.3 us
    all_gather x1, waiting for transfers between devices, body(): lax.all_gather(amplitudes, 'col', axis=1, tiled=True)  88.8 us
    ppermute x4, waiting for transfers between devices, swapped(): return lax.ppermute(value, axis, pairs)  80 us
    dot_general x1, matrix products, contract(): jnp.einsum('ikca,kcjb->ijab', masked, int_piece, preferred_element_type=j...  21.9 us
    all_to_all x3, local copies, waits for them, and re-layouts, body(): lax.all_to_all(shares, 'slab', split_axis=3, concat_axis=2, tiled=True)  20.5 us
    all_to_all x1, blocking collectives, body(): lax.all_to_all(shares, 'slab', split_axis=3, concat_axis=2, tiled=True)  20.4 us
    unnamed x8, local copies, waits for them, and re-layouts  19.5 us
  transfers between devices with their start and end apart: 7, of which 7 were waited for; matrix products, arithmetic and copies ran while one was open for 1% of the time, Pallas kernels for 0%

commit v1 on v0

--- a/solution.py
+++ b/solution.py
@@ -5,6 +5,19 @@
 
 OBLK = 12
 VTILE = 32
+
+
+def ports_choose(arr, chip_axis):
+    extent = lax.axis_size(chip_axis)
+    arrivals = tuple(((w, (w + 1) % extent) for w in range(extent)))
+    stack_in = tuple(((w, (w - 1) % extent) for w in range(extent)))
+    upper, r1 = ([arr], [arr])
+    for _ in range(extent // 2):
+        upper.append(lax.ppermute(upper[-1], axis_name=chip_axis, perm=arrivals))
+    for _ in range((extent - 1) // 2):
+        r1.append(lax.ppermute(r1[-1], chip_axis, stack_in))
+    mid_arr = jnp.concatenate([*upper[::-1], *r1[1:]], 1)
+    return jnp.roll(mid_arr, (lax.axis_index(chip_axis) - extent // 2) * arr.shape[1], 1)
 
 
 def swapped(value, axis, stride):
@@ -56,11 +69,7 @@
     screened = jnp.where(jnp.remainder(parity, 2.0) == 0.0, integrals, jnp.zeros_like(integrals))
     int_whole = lax.all_gather(screened, "row", axis=0, tiled=True)
     cycle_part = contract(
-        lax.all_gather(amplitudes, "col", axis=1, tiled=True),
-        int_whole,
-        i_start,
-        jnp.int32(0),
-        pair_mask,
+        ports_choose(amplitudes, "col"), int_whole, i_start, jnp.int32(0), pair_mask
     )
     shares = lax.psum_scatter(cycle_part, "slab", scatter_dimension=2, tiled=True)
     spread = lax.all_to_all(shares, "slab", split_axis=3, concat_axis=2, tiled=True)

time: 557 us -> 512 us (0.919)
  waiting for transfers between devices: 415 us -> 335 us
  local copies, waits for them, and re-layouts: 68.1 us -> 93.7 us
    ppermute x0 -> x3, waiting for transfers between devices: none -> 103 us  [the longest x2 103 us: ports_choose(): upper.append(lax.ppermute(upper[-1], axis_name=chip_axis, perm=arrivals))]
    all_gather x1, waiting for transfers between devices: 91.3 us -> 0.01 us  [body(): int_whole = lax.all_gather(screened, 'row', axis=0, tiled=True)]
    all_gather x1 -> x0, waiting for transfers between devices: 88.8 us -> none  [body(): lax.all_gather(amplitudes, 'col', axis=1, tiled=True)]
    unnamed x8 -> x13, local copies, waits for them, and re-layouts: 19.5 us -> 41.5 us
  transfers between devices with their start and end apart: 7 -> 9, of which waited for: 7 -> 7; matrix products, arithmetic and copies ran while one was open for 1% -> 5% of each run, Pallas kernels for 0% -> 0%
where the time goes in v1:
time: 512 us; the launch traced here: 511 us
  waiting for transfers between devices  335 us (65%)
  local copies, waits for them, and re-layouts  93.7 us (18%)
  matrix products  25.9 us (5%)
  blocking collectives  20.4 us (4%)
  between operations  13.5 us (3%)
  other arithmetic  12.4 us (2%)
  starting transfers between devices  10.8 us (2%)
    reduce_scatter x1, waiting for transfers between devices, body(): lax.psum_scatter(cycle_part, 'slab', scatter_dimension=2, tiled=True)  152 us
    ppermute x2, waiting for transfers between devices, ports_choose(): upper.append(lax.ppermute(upper[-1], axis_name=chip_axis, perm=arrivals))  103 us
    ppermute x4, waiting for transfers between devices, swapped(): return lax.ppermute(value, axis, pairs)  80.1 us
    unnamed x13, local copies, waits for them, and re-layouts  41.5 us
    dot_general x1, matrix products, contract(): jnp.einsum('ikca,kcjb->ijab', masked, int_piece, preferred_element_type=j...  22 us
    all_to_all x3, local copies, waits for them, and re-layouts, body(): lax.all_to_all(shares, 'slab', split_axis=3, concat_axis=2, tiled=True)  20.6 us
    all_to_all x1, blocking collectives, body(): lax.all_to_all(shares, 'slab', split_axis=3, concat_axis=2, tiled=True)  20.4 us
    reduce_scatter x1, local copies, waits for them, and re-layouts, body(): lax.psum_scatter(cycle_part, 'slab', scatter_dimension=2, tiled=True)  14.2 us
  transfers between devices with their start and end apart: 9, of which 7 were waited for; matrix products, arithmetic and copies ran while one was open for 5% of the time, Pallas kernels for 0%

profile of v1, /device:TPU:0, one launch (start us, length us, event | category | flops | bytes accessed | tf_op | source)
XLA Modules:
  0.0 511.2 jit_solution(4302197141617056113)
XLA Ops:
  6.6 1.0 convolution_bitcast_fusion
  10.4 6.4 %fusion.10 = bf16[12,60,12,128]{3,1,0,2:T(8,128)(2,1)} fusion(bf16[12,60,12,128]{3,1,2,0:T(8,128)(2,1)} %param.5, f32[128]{0:T(128)S(1)} %convolution_bitcast_fusion, f32[12,60,12]{1,0,2:T(8,128)S(1)} %broadcast_add_fusion), kind=kLoop, calls=%fused_computation.13 | loop fusion | flops 9953280 | bytes 4458752 | tf_op jit(solution)/shard_map/jit(_where)/select_n | solution.py:69
  16.9 1.7 collective-permute-start
  18.5 52.6 %collective-permute-done = bf16[12,12,60,128]{3,2,1,0:T(8,128)(2,1)} collective-permute-done((bf16[12,12,60,128]{3,2,1,0:T(8,128)(2,1)S(1)}, bf16[12,12,60,128]{3,2,1,0:T(8,128)(2,1)}, u32[]{:S(2)}, u32[]{:S(2)}) %collective-permute-start) | collective-permute-done | bytes 2211872 | tf_op jit(solution)/shard_map/ppermute | solution.py:16
  71.6 2.8 collective-permute-start.2
  74.8 50.0 %collective-permute-done.1 = bf16[12,12,60,128]{3,2,1,0:T(8,128)(2,1)} collective-permute-done((bf16[12,12,60,128]{3,2,1,0:T(8,128)(2,1)}, bf16[12,12,60,128]{3,2,1,0:T(8,128)(2,1)}, u32[]{:S(2)}, u32[]{:S(2)}) %collective-permute-start.1) | collective-permute-done | bytes 2211872 | tf_op jit(solution)/shard_map/ppermute | solution.py:16
  124.7 3.5 constant_dynamic-update-slice_fusion.7
  128.3 3.6 constant_dynamic-update-slice_fusion.6
  131.9 2.3 constant_dynamic-update-slice_fusion.5
  134.2 3.6 constant_dynamic-update-slice_fusion.4
  137.8 3.6 constant_dynamic-update-slice_fusion.3
  141.3 3.7 constant_dynamic-update-slice_fusion.2
  145.0 2.4 constant_dynamic-update-slice_fusion.1
  147.4 3.6 constant_dynamic-update-slice_fusion
  151.0 22.0 %fusion.11 = f32[12,12,128,128]{2,3,0,1:T(8,128)} fusion(bf16[12,96,60,128]{3,2,1,0:T(8,128)(2,1)} %constant_dynamic-update-slice_fusion, s32[]{:T(128)S(6)} %select_n.113, bf16[12,48]{1,0:T(8,128)(2,1)S(1)} %convolution_convert_fusion, bf16[48,60,12,128]{3,1,0,2:T(8,128)(2,1)} %all-gather.2.cloned.1.call-done), kind=kOutput, calls=%fused_computation.14 | convolution fusion | flops 13607239680 | bytes 28312708 | tf_op jit(solution)/shard_map/ikca,kcjb->ijab/dot_general | solution.py:43
  172.9 12.7 %copy.18 = f32[12,12,128,128]{3,1,0,2:T(8,128)} copy(f32[12,12,128,128]{2,3,0,1:T(8,128)} %fusion.11) | data formatting | bytes 18874368 | tf_op jit(solution)/shard_map/ikca,kcjb->ijab/transpose | solution.py:43
  185.6 151.7 %reduce-scatter.2.cloned.1.call-done = f32[12,12,16,128]{3,1,0,2:T(8,128)} async-done(((f32[12,12,128,128]{3,1,0,2:T(8,128)}), f32[12,12,16,128]{3,1,0,2:T(8,128)}) %reduce-scatter.2.cloned.1.call-update) | async-done | bytes 1179664 | tf_op jit(solution)/shard_map/reduce_scatter | solution.py:74
  337.4 14.2 %copy.19 = f32[12,12,16,128]{2,0,1,3:T(8,128)} copy(f32[12,12,16,128]{3,1,0,2:T(8,128)} %reduce-scatter.2.cloned.1.call-done) | data formatting | bytes 2359296 | tf_op jit(solution)/shard_map/reduce_scatter | solution.py:74
  351.6 8.8 %reshape.121 = f32[8,1,36864]{2,1,0:T(1,128)S(1)} reshape(f32[128,12,12,16]{3,2,1,0:T(8,128)} %bitcast.47) | data formatting | bytes 2359296
  360.4 20.4 %all_to_all.18 = f32[8,1,36864]{2,1,0:T(1,128)S(1)} all-to-all(f32[8,1,36864]{2,1,0:T(1,128)S(1)} %reshape.121), channel_id=1, replica_groups=mesh['row'=4,'col'=4,'slab'=8] {'slab'}, dimensions={0} | all-to-all | bytes 2359296 | tf_op jit(solution)/shard_map/all_to_all | solution.py:75
  381.3 3.4 reduce
  384.7 10.0 %reshape.122 = f32[128,12,12,16]{3,2,1,0:T(8,128)} reshape(f32[8,36864]{1,0:T(8,128)S(1)} %reduce) | data formatting | bytes 2359296
  394.8 13.8 %copy.38 = f32[12,12,16,8,16]{2,3,4,1,0:T(8,128)} copy(f32[12,12,16,8,16]{2,0,1,4,3:T(8,128)} %bitcast.48) | data formatting | bytes 2359296 | tf_op jit(solution)/shard_map/all_to_all | solution.py:75
  408.6 6.2 %all_to_all.16 = f32[12,12,128,16]{2,3,1,0:T(8,128)S(1)} reshape(f32[12,12,8,16,16]{3,2,4,1,0:T(8,128)} %bitcast.49) | data formatting | bytes 2359296 | tf_op jit(solution)/shard_map/all_to_all | solution.py:75
  415.1 2.8 collective-permute-done.3
  417.9 1.5 collective-permute-start.4
  419.4 26.5 %collective-permute-done.4 = f32[12,12,16,128]{3,2,1,0:T(8,128)S(1)} collective-permute-done((f32[12,12,16,128]{3,2,1,0:T(8,128)S(1)}, f32[12,12,16,128]{3,2,1,0:T(8,128)S(1)}, u32[]{:S(2)}, u32[]{:S(2)}) %collective-permute-start.4) | collective-permute-done | bytes 1179680 | tf_op jit(solution)/shard_map/ppermute | solution.py:26
  446.2 1.3 collective-permute-start.5
  447.4 26.0 %collective-permute-done.5 = f32[12,12,16,128]{3,2,1,0:T(8,128)S(1)} collective-permute-done((f32[12,12,16,128]{3,2,1,0:T(8,128)S(1)}, f32[12,12,16,128]{3,2,1,0:T(8,128)S(1)}, u32[]{:S(2)}, u32[]{:S(2)}) %collective-permute-start.5) | collective-permute-done | bytes 1179680 | tf_op jit(solution)/shard_map/ppermute | solution.py:26
  473.4 3.0 collective-permute-start.6
  476.4 24.8 %collective-permute-done.6 = f32[12,12,16,128]{3,2,1,0:T(8,128)S(1)} collective-permute-done((f32[12,12,16,128]{3,2,1,0:T(8,128)S(1)}, f32[12,12,16,128]{3,2,1,0:T(8,128)S(1)}, u32[]{:S(2)}, u32[]{:S(2)}) %collective-permute-start.6) | collective-permute-done | bytes 1179680 | tf_op jit(solution)/shard_map/ppermute | solution.py:26
  501.2 2.2 fusion.16
  (28 shorter events, 5.6 us)
Async XLA Ops:
  6.5 10.3 %copy-start = (bf16[12,12,60,128]{3,2,1,0:T(8,128)(2,1)S(1)}, bf16[12,12,60,128]{3,2,1,0:T(8,128)(2,1)}, u32[]{:S(2)}) copy-start(bf16[12,12,60,128]{3,2,1,0:T(8,128)(2,1)} %param.4) | copy-start | bytes 6635524
  6.5 67.9 %copy-start.1 = (s32[4,4]{1,0:T(4,128)S(1)}, s32[4,4]{1,0:T(4,128)}, u32[]{:S(2)}) copy-start(s32[4,4]{1,0:T(4,128)} %param.7) | copy-start | bytes 196
  6.5 144.4 %all-gather.2.cloned.1.call-start = ((), (), s32[]{:S(2)}) async-start(), calls=%async_computation.2 | async-start | bytes 11796480 | tf_op jit(solution)/shard_map/all_gather | solution.py:70
  16.8 320.6 %reduce-scatter.2.cloned.1.call-start = ((), (), s32[]{:S(2)}) async-start(), calls=%async_computation.3 | async-start | bytes 14155776 | tf_op jit(solution)/shard_map/reduce_scatter | solution.py:74
  16.9 54.3 %collective-permute-start = (bf16[12,12,60,128]{3,2,1,0:T(8,128)(2,1)S(1)}, bf16[12,12,60,128]{3,2,1,0:T(8,128)(2,1)}, u32[]{:S(2)}, u32[]{:S(2)}) collective-permute-start(bf16[12,12,60,128]{3,2,1,0:T(8,128)(2,1)S(1)} %copy-done), channel_id=1, source_target_pairs={{0,8},{8,16},{16,24},{24,0},{1,9},{9,17},{17,25},{25,1},{2,10},{10... | collective-permute-start | bytes 6635528 | tf_op jit(solution)/shard_map/ppermute | solution.py:16
  71.2 53.6 %collective-permute-start.1 = (bf16[12,12,60,128]{3,2,1,0:T(8,128)(2,1)}, bf16[12,12,60,128]{3,2,1,0:T(8,128)(2,1)}, u32[]{:S(2)}, u32[]{:S(2)}) collective-permute-start(bf16[12,12,60,128]{3,2,1,0:T(8,128)(2,1)} %collective-permute-done), channel_id=1, source_target_pairs={{0,8},{8,16},{16,24},{24,0},{1,9},{9,17},{17,25},{25,1},{2,10},{10... | collective-permute-start | bytes 6635528 | tf_op jit(solution)/shard_map/ppermute | solution.py:16
  71.6 62.5 %collective-permute-start.2 = (bf16[12,12,60,128]{3,2,1,0:T(8,128)(2,1)S(1)}, bf16[12,12,60,128]{3,2,1,0:T(8,128)(2,1)}, u32[]{:S(2)}, u32[]{:S(2)}) collective-permute-start(bf16[12,12,60,128]{3,2,1,0:T(8,128)(2,1)S(1)} %copy-done), channel_id=1, source_target_pairs={{0,24},{8,0},{16,8},{24,16},{1,25},{9,1},{17,9},{25,17},{2,26},{10... | collective-permute-start | bytes 6635528 | tf_op jit(solution)/shard_map/ppermute | solution.py:18
  415.0 2.9 collective-permute-start.3
  417.9 28.0 %collective-permute-start.4 = (f32[12,12,16,128]{3,2,1,0:T(8,128)S(1)}, f32[12,12,16,128]{3,2,1,0:T(8,128)S(1)}, u32[]{:S(2)}, u32[]{:S(2)}) collective-permute-start(f32[12,12,16,128]{3,2,1,0:T(8,128)S(1)} %collective-permute-done.3), channel_id=1, source_target_pairs={{0,8},{8,0},{16,24},{24,16},{1,9},{9,1},{17,25},{25,17},{2,10},{10... | collective-permute-start | bytes 3538952 | tf_op jit(solution)/shard_map/ppermute | solution.py:26
  446.2 27.2 %collective-permute-start.5 = (f32[12,12,16,128]{3,2,1,0:T(8,128)S(1)}, f32[12,12,16,128]{3,2,1,0:T(8,128)S(1)}, u32[]{:S(2)}, u32[]{:S(2)}) collective-permute-start(f32[12,12,16,128]{3,2,1,0:T(8,128)S(1)} %copy.23), channel_id=1, source_target_pairs={{0,64},{32,96},{64,0},{96,32},{1,65},{33,97},{65,1},{97,33},{2,66}... | collective-permute-start | bytes 3538952 | tf_op jit(solution)/shard_map/ppermute | solution.py:26
  473.4 27.8 %collective-permute-start.6 = (f32[12,12,16,128]{3,2,1,0:T(8,128)S(1)}, f32[12,12,16,128]{3,2,1,0:T(8,128)S(1)}, u32[]{:S(2)}, u32[]{:S(2)}) collective-permute-start(f32[12,12,16,128]{3,2,1,0:T(8,128)S(1)} %collective-permute-done.5), channel_id=1, source_target_pairs={{0,16},{8,24},{16,0},{24,8},{1,17},{9,25},{17,1},{25,9},{2,18},{10... | collective-permute-start | bytes 3538952 | tf_op jit(solution)/shard_map/ppermute | solution.py:26
Sparse Core Ops, SparseCore 0:
  16.9 91.0 all-gather.1
  185.8 151.5 reduce-scatter.1
